TPU v7x, 32 devices: a whole 2x2x4 slice. The times are simulated.
32 devices in a mesh: group: 4 (over y, core), gx: 4 (over z), gy: 2 (over x).
Axes of the slice: x: 2, y: 2, z: 4, core: 2. Of those that a mesh axis runs over, the one named last changes fastest.
Arguments:
- populations: bfloat16 [19, 32, 16, 128], P(None, ('group', 'gx'), 'gy'), may hold values from 0 to 1, as said below
- solid_mask: int32 [32, 16, 128], P(('group', 'gx'), 'gy'), may hold values 0 or 1
- wall_cells: int32 [16, 2, 512], P(('group', 'gx'), 'gy'), may hold values from 0 to 2047
- body_load: float32 [3, 64, 8, 128], P(None, ('group', 'gx'), 'gy'), may hold values from -3 to 3
- elem_scale: float32 [64, 8, 128], P(('group', 'gx'), 'gy'), may hold values from 0.05 to 0.5
- elem_active: int32 [64, 8, 128], P(('group', 'gx'), 'gy'), may hold values 0 or 1
- elem_matrix: float32 [24, 24], replicated, may hold values from -0.25 to 8, as said below
- iface_nodes: int32 [16, 2, 256], P(('group', 'gx'), 'gy'), may hold values from 0 to 2047
- iface_coords: float32 [3, 16, 2, 256], P(None, ('group', 'gx'), 'gy'), may hold values from 0 to 128
- neighbours: int32 [16, 2, 2, 8], P(('group', 'gx'), 'gy'), may hold values from 0 to 11, as said below
Outputs:
- new_populations: bfloat16 [19, 32, 16, 128], P(None, ('group', 'gx'), 'gy')
- displacement: float32 [3, 64, 8, 128], P(None, ('group', 'gx'), 'gy')
Inputs may be any that keep to these rules, and one draw needn't show every extreme that they name: `populations`: each population is positive, between 0.48 and 1.68 times its lattice weight. `elem_matrix`: symmetric. `neighbours`: on devices of structure group 3 + j every entry is g * 4 + t with t < 4, g < 3 and g congruent to j modulo 1.
All inputs are finite; a program needn't handle non-finite values. No bound on the sum of `solid_mask` or of `elem_active` on one device may be relied on, other than what follows from the above.
Results may differ from a plain program's by a relative error of at most 0.0019.
Values may be sent and summed in bfloat16 or wider, within the bound.
No kernel may reach another device: no remote copies, remote signals or barrier semaphores. Data moves between devices by JAX's collectives and lax.ppermute only.
A program may use at most 64 MiB of HBM per device.

v0:
```python
import jax
import jax.numpy as jnp
from jax import lax
from jax.sharding import PartitionSpec as P

TILE = 128
ITERS = 3
velocity = [
    (0, 0, 0),
    (1, 0, 0),
    (-1, 0, 0),
    (0, 1, 0),
    (0, -1, 0),
    (0, 0, 1),
    (0, 0, -1),
    (1, 1, 0),
    (-1, -1, 0),
    (1, -1, 0),
    (-1, 1, 0),
    (1, 0, 1),
    (-1, 0, -1),
    (1, 0, -1),
    (-1, 0, 1),
    (0, 1, 1),
    (0, -1, -1),
    (0, 1, -1),
    (0, -1, 1),
]
opposite = [0, 2, 1, 4, 3, 6, 5, 8, 7, 10, 9, 12, 11, 14, 13, 16, 15, 18, 17]
lattice_weight = [1.0 / 3.0] + [1.0 / 18.0] * 6 + [1.0 / 36.0] * 12
relax_rate = 1.0 / 0.6
wall_gain = 60.0
basis_radius = 24.0
mass_shift = 0.5


def padded(cells, sides, width):
    for axis, dim in sides:
        count = lax.axis_size(axis)
        ends = count - 1
        head = lax.slice_in_dim(cells, 0, width, axis=dim)
        tail = lax.slice_in_dim(cells, cells.shape[dim] - width, cells.shape[dim], axis=dim)
        cells = jnp.concatenate(
            [
                lax.ppermute(tail, axis, [(i, (i + 1) % count) for i in range(ends)]),
                cells,
                lax.ppermute(head, axis, [((i + 1) % count, i) for i in range(ends)]),
            ],
            axis=dim,
        )
    return cells


def passed_along(value, axis, steps):
    count = lax.axis_size(axis)
    pairs = [(source, (source + steps) % count) for source in range(count)]
    return lax.ppermute(value, axis, pairs)


def project_onto(vectors, direction):
    summed = jnp.zeros_like(vectors[0])
    for component in range(3):
        if direction[component] != 0:
            summed = summed + float(direction[component]) * vectors[component]
    return summed


def collide(population):
    density = jnp.sum(population, axis=0)
    momentum = [jnp.zeros_like(density) for component in range(3)]
    for q in range(19):
        for component in range(3):
            if velocity[q][component] != 0:
                momentum[component] = (
                    momentum[component] + float(velocity[q][component]) * population[q]
                )
    velocity_parts = [entry / density for entry in momentum]
    speed_square = (
        velocity_parts[0] * velocity_parts[0]
        + velocity_parts[1] * velocity_parts[1]
        + velocity_parts[2] * velocity_parts[2]
    )
    relaxed = []
    for q in range(19):
        project = project_onto(velocity_parts, velocity[q])
        balance = (
            lattice_weight[q]
            * density
            * (1.0 + 3.0 * project + 4.5 * project * project - 1.5 * speed_square)
        )
        relaxed.append(population[q] + relax_rate * (balance - population[q]))
    return jnp.stack(relaxed)


def stream_links(moved, fluid_ext):
    span_cells = moved.shape[1] - 2
    across_cells = moved.shape[2] - 2
    deep_cells = moved.shape[3] - 2
    upstream, opened, bounce, reflected = ([], [], [], [])
    for q in range(19):
        shift_x, shift_y, shift_z = velocity[q]
        window = (
            slice(1 - shift_x, 1 - shift_x + span_cells),
            slice(1 - shift_y, 1 - shift_y + across_cells),
            slice(1 - shift_z, 1 - shift_z + deep_cells),
        )
        upstream.append(moved[q][window])
        open_up = fluid_ext[window]
        opened.append(open_up)
        bounce.append(1.0 - open_up)
        reflected.append(
            moved[opposite[q], 1 : span_cells + 1, 1 : across_cells + 1, 1 : deep_cells + 1]
        )
    return (upstream, opened, bounce, reflected)


def wall_force(bounce, reflected):
    force_parts = [jnp.zeros_like(reflected[0]) for component in range(3)]
    for q in range(19):
        for component in range(3):
            if velocity[q][component] != 0:
                force_parts[component] = (
                    force_parts[component]
                    - 2.0 * float(velocity[q][component]) * bounce[q] * reflected[q]
                )
    return jnp.stack(force_parts)


def stream_all(moved, fluid_ext, wall_speed):
    upstream, opened, bounce, reflected = stream_links(moved, fluid_ext)
    inside = fluid_ext[1:-1, 1:-1, 1:-1]
    speed_list = [wall_speed[0], wall_speed[1], wall_speed[2]]
    result = []
    for q in range(19):
        correction = 6.0 * lattice_weight[q] * project_onto(speed_list, velocity[q])
        result.append(inside * (opened[q] * upstream[q] + bounce[q] * (reflected[q] + correction)))
    return jnp.stack(result).astype(jnp.bfloat16)


def basis_weights(received, node_positions, tile_lists):
    tile_count = tile_lists.shape[0]
    tile_width = received.shape[2]
    chosen = received[tile_lists]
    nodes_at = node_positions.reshape(3, tile_count, tile_width)
    distance = jnp.zeros((tile_count, tile_width, tile_lists.shape[1], tile_width), jnp.float32)
    for component in range(3):
        offset = nodes_at[component][:, :, None, None] - chosen[:, None, :, 3 + component, :]
        distance = distance + offset * offset
    kernel = 1.0 / jnp.sqrt(1.0 + distance / (basis_radius * basis_radius))
    column = jnp.sum(kernel, axis=1)
    totals = (
        jnp.zeros((received.shape[0], tile_width), jnp.float32)
        .at[tile_lists.reshape(-1)]
        .add(column.reshape(-1, tile_width))
    )
    return (kernel / totals[tile_lists][:, None, :, :], chosen)


def map_tractions(weights, chosen, node_index, nodes_total):
    mapped = jnp.einsum(
        "anbp,abcp->can", weights, chosen[:, :, 0:3, :], precision=lax.Precision.HIGHEST
    )
    return jnp.zeros((3, nodes_total), jnp.float32).at[:, node_index].add(mapped.reshape(3, -1))


def map_speeds(weights, solution_flat, node_index, tile_lists, tile_slots):
    tile_count = weights.shape[0]
    tile_width = weights.shape[1]
    at_nodes = solution_flat[:, node_index].reshape(3, tile_count, tile_width)
    contrib = jnp.einsum("anbp,can->abcp", weights, at_nodes, precision=lax.Precision.HIGHEST)
    return (
        jnp.zeros((tile_slots, 3, tile_width), jnp.float32)
        .at[tile_lists.reshape(-1)]
        .add(contrib.reshape(-1, 3, tile_width))
    )


def element_sum(widened, matrix):
    span_cells = widened.shape[1] - 2
    across_cells = widened.shape[2] - 2
    deep_cells = widened.shape[3]
    widened_z = jnp.pad(widened, ((0, 0), (0, 0), (0, 0), (0, 1)))
    corners = [(a, b, c) for a in (0, 1) for b in (0, 1) for c in (0, 1)]
    gathered = jnp.concatenate(
        [
            widened_z[0:3, a : a + span_cells + 1, b : b + across_cells + 1, c : c + deep_cells]
            for a, b, c in corners
        ],
        axis=0,
    )
    element_scale = widened_z[3, 0 : span_cells + 1, 0 : across_cells + 1, 0:deep_cells]
    forces = element_scale * jnp.einsum(
        "ij,jabc->iabc", matrix, gathered, precision=lax.Precision.HIGHEST
    )
    summed = jnp.zeros((3, span_cells + 2, across_cells + 2, deep_cells + 1), jnp.float32)
    for corner_id, (a, b, c) in enumerate(corners):
        summed = summed.at[
            :, a : a + span_cells + 1, b : b + across_cells + 1, c : c + deep_cells
        ].add(forces[3 * corner_id : 3 * corner_id + 3])
    return summed[:, 1 : span_cells + 1, 1 : across_cells + 1, 0:deep_cells]


def apply_operator(values, stiffness, is_struct, matrix):
    stacked = jnp.concatenate([values, stiffness[None]], axis=0)
    widened = padded(stacked, (("gx", 1), ("gy", 2)), 1)

    def active_side(operands):
        return mass_shift * operands[2] + element_sum(operands[0], operands[1])

    def quiet_side(operands):
        return jnp.zeros_like(operands[2])

    return lax.cond(is_struct, active_side, quiet_side, (widened, matrix, values))


def global_products(first_vec, second_vec):
    return lax.psum(
        (jnp.sum(first_vec * first_vec), jnp.sum(first_vec * second_vec)), ("group", "gx", "gy")
    )


def solve_structure(right_side, operator, products):
    residual = right_side
    image_vec = operator(residual)
    norm_now, curvature = products(residual, image_vec)
    step_size = norm_now / curvature
    direction, image_dir = (residual, image_vec)
    solution = jnp.zeros_like(right_side)
    for iteration in range(ITERS):
        solution = solution + step_size * direction
        residual = residual - step_size * image_dir
        if iteration + 1 < ITERS:
            image_vec = operator(residual)
            norm_next, curvature = products(residual, image_vec)
            beta_ratio = norm_next / norm_now
            step_size = norm_next / (curvature - beta_ratio * norm_next / step_size)
            direction = residual + beta_ratio * direction
            image_dir = image_vec + beta_ratio * image_dir
            norm_now = norm_next
    return solution


def per_device(
    populations,
    solid_mask,
    wall_cells,
    body_load,
    elem_scale,
    elem_active,
    elem_matrix,
    iface_nodes,
    iface_coords,
    neighbours,
):
    group_count = lax.axis_size("group")
    span_devices = lax.axis_size("gx")
    struct_groups = max(1, group_count // 8)
    fluid_groups = group_count - struct_groups
    group_index = lax.axis_index("group")
    slab_index = group_index * span_devices + lax.axis_index("gx")
    column_index = lax.axis_index("gy")
    is_fluid = group_index < fluid_groups
    is_struct = jnp.logical_not(is_fluid)
    span_cells, across_cells, deep_cells = solid_mask.shape
    cell_count = span_cells * across_cells * deep_cells
    fluid_here = jnp.where(is_fluid, 1.0 - solid_mask.astype(jnp.float32), 0.0)
    relaxed_pops = lax.cond(
        is_fluid,
        lambda pops: collide(pops.astype(jnp.float32)).astype(jnp.bfloat16),
        lambda pops: jnp.zeros_like(pops),
        populations,
    )
    marker = fluid_here.astype(jnp.bfloat16)[None]
    widened = padded(
        jnp.concatenate([relaxed_pops, marker], axis=0), ((("group", "gx"), 1), ("gy", 2)), 1
    )
    widened = jnp.pad(widened, ((0, 0), (0, 0), (0, 0), (1, 1))).astype(jnp.float32)
    moved = widened[0:19]
    fluid_ext = widened[19]
    wall_index = wall_cells.reshape(-1)
    point_count = wall_index.shape[0]
    tiles_out = point_count // TILE

    def fluid_pack(operands):
        upstream, opened, bounce, reflected = stream_links(operands[0], operands[1])
        force_parts = wall_force(bounce, reflected).reshape(3, cell_count)
        picked = force_parts[:, wall_index]
        span_pos = wall_index // (across_cells * deep_cells)
        across_pos = wall_index // deep_cells % across_cells + column_index * across_cells
        deep_pos = wall_index % deep_cells
        positions = jnp.stack(
            [
                (slab_index * span_cells + span_pos).astype(jnp.float32),
                across_pos.astype(jnp.float32),
                deep_pos.astype(jnp.float32),
            ]
        )
        packed = jnp.concatenate([picked, positions], axis=0)
        return packed.reshape(6, tiles_out, TILE).transpose(1, 0, 2)

    packed = lax.cond(
        is_fluid,
        fluid_pack,
        lambda operands: jnp.zeros((tiles_out, 6, TILE), jnp.float32),
        (moved, fluid_ext),
    )
    received = lax.all_gather(packed, "group", axis=0, tiled=True)
    node_index = iface_nodes.reshape(-1)
    node_positions = iface_coords.reshape(3, -1)
    tile_lists = neighbours.reshape(neighbours.shape[2], neighbours.shape[3])
    nodes_total = body_load.shape[1] * body_load.shape[2] * body_load.shape[3]
    weight_shape = (tile_lists.shape[0], TILE, tile_lists.shape[1], TILE)

    def struct_map(received_all):
        weights, chosen = basis_weights(received_all, node_positions, tile_lists)
        mapped = map_tractions(weights, chosen, node_index, nodes_total)
        return (weights, body_load + mapped.reshape(body_load.shape))

    def struct_quiet(received_all):
        return (jnp.zeros(weight_shape, jnp.float32), jnp.zeros_like(body_load))

    weights, right_side = lax.cond(is_struct, struct_map, struct_quiet, received)
    stiffness = jnp.where(is_struct, elem_scale * elem_active.astype(jnp.float32), 0.0)
    solution = solve_structure(
        right_side,
        lambda values: apply_operator(values, stiffness, is_struct, elem_matrix),
        global_products,
    )
    tile_slots = received.shape[0]

    def struct_back(operands):
        return map_speeds(
            operands[0], operands[1].reshape(3, nodes_total), node_index, tile_lists, tile_slots
        )

    back_terms = lax.cond(
        is_struct,
        struct_back,
        lambda operands: jnp.zeros((tile_slots, 3, TILE), jnp.float32),
        (weights, solution),
    )
    per_group = tile_slots // group_count
    route_count = fluid_groups // struct_groups
    sender_slot = jnp.clip(group_index - fluid_groups, 0, struct_groups - 1)
    own_speeds = jnp.zeros((per_group, 3, TILE), jnp.float32)
    for route_step in range(route_count):
        offset_row = (sender_slot + route_step * struct_groups) * per_group
        outgoing = lax.dynamic_slice_in_dim(back_terms, offset_row, per_group, 0)
        incoming = passed_along(outgoing, "group", (route_step + 1) * struct_groups)
        own_speeds = own_speeds + jnp.where(
            group_index // struct_groups == route_step, incoming, 0.0
        )
    speed_parts = wall_gain * own_speeds.transpose(1, 0, 2).reshape(3, point_count)
    wall_speed = jnp.zeros((3, cell_count), jnp.float32).at[:, wall_index].add(speed_parts)
    wall_speed = wall_speed.reshape(3, span_cells, across_cells, deep_cells)
    new_populations = lax.cond(
        is_fluid,
        lambda operands: stream_all(operands[0], operands[1], operands[2]),
        lambda operands: jnp.zeros(operands[0][:, 1:-1, 1:-1, 1:-1].shape, jnp.bfloat16),
        (moved, fluid_ext, wall_speed),
    )
    return (new_populations, solution)


def solution(mesh):
    placed = (
        P(None, ("group", "gx"), "gy", None),
        P(("group", "gx"), "gy", None),
        P(("group", "gx"), "gy", None),
        P(None, ("group", "gx"), "gy", None),
        P(("group", "gx"), "gy", None),
        P(("group", "gx"), "gy", None),
        P(),
        P(("group", "gx"), "gy", None),
        P(None, ("group", "gx"), "gy", None),
        P(("group", "gx"), "gy", None, None),
    )
    return jax.shard_map(
        per_device,
        mesh=mesh,
        in_specs=placed,
        out_specs=(P(None, ("group", "gx"), "gy", None), P(None, ("group", "gx"), "gy", None)),
        check_vma=False,
    )
```

profile of v0, /device:TPU:1, one launch (start us, length us, event | category | flops | bytes accessed | tf_op | source)
XLA Modules:
  0.0 306.8 jit_solution(16468863628029610171)
XLA Ops:
  1.4 13.3 %conditional.8 = (bf16[19,2,8,128]{3,2,1,0:T(8,128)(2,1)}) conditional(s32[]{:T(128)} %convert_element_type.59, () %tuple.155, (bf16[19,2,8,128]{3,2,1,0:T(8,128)(2,1)}) %tuple.170), branch_computations={%region_0.1_spmd, %region_1.3_spmd} | conditional | flops 724991 | bytes 1282056 | solution.py:267
  15.5 4.0 %collective-permute-start = (bf16[20,1,8,128]{3,2,1,0:T(8,128)(2,1)S(1)}, bf16[20,1,8,128]{3,2,1,0:T(8,128)(2,1)S(1)}, u32[]{:S(2)}, u32[]{:S(2)}) collective-permute-start(bf16[20,1,8,128]{3,2,1,0:T(8,128)(2,1)S(1)} %get-tuple-element.547), channel_id=1, source_target_pairs={{0,2},{2,4},{4,6},{6,8},{8,10},{10,12},{12,14},{14,16},{16,18},{18... | collective-permute-start | bytes 122888 | tf_op jit(solution)/shard_map/ppermute | solution.py:45
  19.5 4.5 %collective-permute-start.1 = (bf16[20,1,8,128]{3,2,1,0:T(8,128)(2,1)S(1)}, bf16[20,1,8,128]{3,2,1,0:T(8,128)(2,1)S(1)}, u32[]{:S(2)}, u32[]{:S(2)}) collective-permute-start(bf16[20,1,8,128]{3,2,1,0:T(8,128)(2,1)S(1)} %get-tuple-element.548), channel_id=1, source_target_pairs={{2,0},{4,2},{6,4},{8,6},{10,8},{12,10},{14,12},{16,14},{18,16},{20... | collective-permute-start | bytes 122888 | tf_op jit(solution)/shard_map/ppermute | solution.py:47
  26.2 3.1 %collective-permute-start.2 = (bf16[20,4,1,128]{3,2,1,0:T(2,128)(2,1)S(1)}, bf16[20,4,1,128]{3,2,1,0:T(2,128)(2,1)S(1)}, u32[]{:S(2)}, u32[]{:S(2)}) collective-permute-start(bf16[20,4,1,128]{3,2,1,0:T(2,128)(2,1)S(1)} %get-tuple-element.545), channel_id=1, source_target_pairs={{0,1},{2,3},{4,5},{6,7},{8,9},{10,11},{12,13},{14,15},{16,17},{18,... | collective-permute-start | bytes 61448 | tf_op jit(solution)/shard_map/ppermute | solution.py:45
  30.6 3.4 %collective-permute-done.3 = bf16[20,4,1,128]{3,2,1,0:T(2,128)(2,1)S(1)} collective-permute-done((bf16[20,4,1,128]{3,2,1,0:T(2,128)(2,1)S(1)}, bf16[20,4,1,128]{3,2,1,0:T(2,128)(2,1)S(1)}, u32[]{:S(2)}, u32[]{:S(2)}) %collective-permute-start.3) | collective-permute-done | bytes 20512 | tf_op jit(solution)/shard_map/ppermute | solution.py:47
  38.2 7.8 %all_gather.3 = f32[16,6,128]{2,1,0:T(8,128)S(1)} all-gather(f32[4,6,128]{2,1,0:T(8,128)S(1)} %copy.69), channel_id=1, replica_groups=mesh['group'=4,'gx'=4,'gy'=2] {'group'}, dimensions={0}, use_global_device_ids=true | all-gather | bytes 61440 | tf_op jit(solution)/shard_map/all_gather | solution.py:307
  47.6 3.2 %collective-permute-start.4 = (f32[4,1,4,128]{3,0,2,1:T(4,128)S(1)}, f32[4,1,4,128]{3,0,2,1:T(4,128)S(1)}, u32[]{:S(2)}, u32[]{:S(2)}) collective-permute-start(f32[4,1,4,128]{3,0,2,1:T(4,128)S(1)} %get-tuple-element.555), channel_id=1, source_target_pairs={{0,2},{2,4},{4,6},{1,3},{3,5},{5,7},{8,10},{10,12},{12,14},{9,11},... | collective-permute-start | bytes 24584 | tf_op jit(solution)/shard_map/ppermute | solution.py:45
  52.1 3.1 %collective-permute-done.5 = f32[4,1,4,128]{3,0,2,1:T(4,128)S(1)} collective-permute-done((f32[4,1,4,128]{3,0,2,1:T(4,128)S(1)}, f32[4,1,4,128]{3,0,2,1:T(4,128)S(1)}, u32[]{:S(2)}, u32[]{:S(2)}) %collective-permute-start.5) | collective-permute-done | bytes 8224 | tf_op jit(solution)/shard_map/ppermute | solution.py:47
  58.7 2.3 collective-permute-done.7
  62.0 65.4 %all-reduce.9 = (f32[]{:T(128)}, f32[]{:T(128)}) all-reduce(f32[]{:T(128)} %multiply_reduce_fusion, f32[]{:T(128)} %multiply_reduce_fusion.1), channel_id=1, replica_groups=mesh['group'=4,'gx'=4,'gy'=2] {'group','gx','gy'}, use_global_device_ids=true, to_apply=%region_11.12 | all-reduce | flops 2 | bytes 16 | tf_op jit(solution)/shard_map/psum | solution.py:217
  128.8 2.1 collective-permute-start.8
  132.2 3.1 %collective-permute-done.9 = f32[4,1,4,128]{3,2,1,0:T(4,128)S(1)} collective-permute-done((f32[4,1,4,128]{3,2,1,0:T(4,128)S(1)}, f32[4,1,4,128]{3,2,1,0:T(4,128)S(1)}, u32[]{:S(2)}, u32[]{:S(2)}) %collective-permute-start.9) | collective-permute-done | bytes 8224 | tf_op jit(solution)/shard_map/ppermute | solution.py:47
  135.3 2.6 collective-permute-start.10
  139.2 3.1 %collective-permute-done.11 = f32[4,6,1,128]{3,2,1,0:T(1,128)S(1)} collective-permute-done((f32[4,6,1,128]{3,2,1,0:T(1,128)S(1)}, f32[4,6,1,128]{3,2,1,0:T(1,128)S(1)}, u32[]{:S(2)}, u32[]{:S(2)}) %collective-permute-start.11) | collective-permute-done | bytes 12320 | tf_op jit(solution)/shard_map/ppermute | solution.py:47
  143.3 55.8 %all-reduce.8 = (f32[]{:T(128)}, f32[]{:T(128)}) all-reduce(f32[]{:T(128)} %get-tuple-element.478, f32[]{:T(128)} %get-tuple-element.477), channel_id=1, replica_groups=mesh['group'=4,'gx'=4,'gy'=2] {'group','gx','gy'}, use_global_device_ids=true, to_apply=%region_17.18 | all-reduce | flops 2 | bytes 16 | tf_op jit(solution)/shard_map/psum | solution.py:217
  203.7 2.2 collective-permute-start.12
  207.2 3.1 %collective-permute-done.13 = f32[4,1,4,128]{3,2,1,0:T(4,128)S(1)} collective-permute-done((f32[4,1,4,128]{3,2,1,0:T(4,128)S(1)}, f32[4,1,4,128]{3,2,1,0:T(4,128)S(1)}, u32[]{:S(2)}, u32[]{:S(2)}) %collective-permute-start.13) | collective-permute-done | bytes 8224 | tf_op jit(solution)/shard_map/ppermute | solution.py:47
  210.4 2.5 collective-permute-start.14
  214.2 3.1 %collective-permute-done.15 = f32[4,6,1,128]{3,2,1,0:T(1,128)S(1)} collective-permute-done((f32[4,6,1,128]{3,2,1,0:T(1,128)S(1)}, f32[4,6,1,128]{3,2,1,0:T(1,128)S(1)}, u32[]{:S(2)}, u32[]{:S(2)}) %collective-permute-start.15) | collective-permute-done | bytes 12320 | tf_op jit(solution)/shard_map/ppermute | solution.py:47
  218.0 55.8 %all-reduce.7 = (f32[]{:T(128)}, f32[]{:T(128)}) all-reduce(f32[]{:T(128)} %get-tuple-element.476, f32[]{:T(128)} %get-tuple-element.475), channel_id=1, replica_groups=mesh['group'=4,'gx'=4,'gy'=2] {'group','gx','gy'}, use_global_device_ids=true, to_apply=%region_23.24 | all-reduce | flops 2 | bytes 16 | tf_op jit(solution)/shard_map/psum | solution.py:217
  279.8 3.4 %collective-permute-start.16 = (f32[4,3,128]{2,1,0:T(4,128)S(1)}, f32[4,3,128]{2,1,0:T(4,128)S(1)}, u32[]{:S(2)}, u32[]{:S(2)}) collective-permute-start(f32[4,3,128]{2,1,0:T(4,128)S(1)} %get-tuple-element.557), channel_id=1, source_target_pairs={{0,8},{8,16},{16,24},{24,0},{1,9},{9,17},{17,25},{25,1},{2,10},{10... | collective-permute-start | bytes 18440 | tf_op jit(solution)/shard_map/ppermute | solution.py:57
  283.1 3.3 %collective-permute-start.17 = (f32[4,3,128]{2,1,0:T(4,128)S(1)}, f32[4,3,128]{2,1,0:T(4,128)S(1)}, u32[]{:S(2)}, u32[]{:S(2)}) collective-permute-start(f32[4,3,128]{2,1,0:T(4,128)S(1)} %get-tuple-element.559), channel_id=1, source_target_pairs={{0,16},{8,24},{16,0},{24,8},{1,17},{9,25},{17,1},{25,9},{2,18},{10... | collective-permute-start | bytes 18440 | tf_op jit(solution)/shard_map/ppermute | solution.py:57
  289.7 2.5 scatter_custom_fusion.3
  292.2 14.7 %conditional.15 = (bf16[19,2,8,128]{3,2,1,0:T(8,128)(2,1)}) conditional(s32[]{:T(128)} %convert_element_type.59, () %tuple.154, (f32[4,10,130]{2,1,0:T(8,128)S(1)}, f32[19,4,10,130]{3,2,1,0:T(8,128)S(1)}, f32[3,2048]{0,1:T(8,128)S(1)}) %tuple.168), branch_computations={%region_32.33_spmd, %region_33.34_spmd} | conditional | flops 356351 | bytes 1826696 | solution.py:356
  (135 shorter events, 60.2 us)
Async XLA Ops:
  0.6 30.0 %copy-start.3 = (f32[4,4,128]{2,1,0:T(4,128)S(1)}, f32[4,4,128]{2,1,0:T(4,128)}, u32[]{:S(2)}) copy-start(f32[4,4,128]{2,1,0:T(4,128)} %param.78) | copy-start | bytes 24580
  0.6 30.0 %copy-start.4 = (s32[4,4,128]{2,1,0:T(4,128)S(1)}, s32[4,4,128]{2,1,0:T(4,128)}, u32[]{:S(2)}) copy-start(s32[4,4,128]{2,1,0:T(4,128)} %param.79) | copy-start | bytes 24580
  15.5 8.6 %collective-permute-start = (bf16[20,1,8,128]{3,2,1,0:T(8,128)(2,1)S(1)}, bf16[20,1,8,128]{3,2,1,0:T(8,128)(2,1)S(1)}, u32[]{:S(2)}, u32[]{:S(2)}) collective-permute-start(bf16[20,1,8,128]{3,2,1,0:T(8,128)(2,1)S(1)} %get-tuple-element.547), channel_id=1, source_target_pairs={{0,2},{2,4},{4,6},{6,8},{8,10},{10,12},{12,14},{14,16},{16,18},{18... | collective-permute-start | bytes 122888 | tf_op jit(solution)/shard_map/ppermute | solution.py:45
  19.5 5.6 %collective-permute-start.1 = (bf16[20,1,8,128]{3,2,1,0:T(8,128)(2,1)S(1)}, bf16[20,1,8,128]{3,2,1,0:T(8,128)(2,1)S(1)}, u32[]{:S(2)}, u32[]{:S(2)}) collective-permute-start(bf16[20,1,8,128]{3,2,1,0:T(8,128)(2,1)S(1)} %get-tuple-element.548), channel_id=1, source_target_pairs={{2,0},{4,2},{6,4},{8,6},{10,8},{12,10},{14,12},{16,14},{18,16},{20... | collective-permute-start | bytes 122888 | tf_op jit(solution)/shard_map/ppermute | solution.py:47
  26.2 4.5 %collective-permute-start.2 = (bf16[20,4,1,128]{3,2,1,0:T(2,128)(2,1)S(1)}, bf16[20,4,1,128]{3,2,1,0:T(2,128)(2,1)S(1)}, u32[]{:S(2)}, u32[]{:S(2)}) collective-permute-start(bf16[20,4,1,128]{3,2,1,0:T(2,128)(2,1)S(1)} %get-tuple-element.545), channel_id=1, source_target_pairs={{0,1},{2,3},{4,5},{6,7},{8,9},{10,11},{12,13},{14,15},{16,17},{18,... | collective-permute-start | bytes 61448 | tf_op jit(solution)/shard_map/ppermute | solution.py:45
  29.3 4.7 %collective-permute-start.3 = (bf16[20,4,1,128]{3,2,1,0:T(2,128)(2,1)S(1)}, bf16[20,4,1,128]{3,2,1,0:T(2,128)(2,1)S(1)}, u32[]{:S(2)}, u32[]{:S(2)}) collective-permute-start(bf16[20,4,1,128]{3,2,1,0:T(2,128)(2,1)S(1)} %get-tuple-element.546), channel_id=1, source_target_pairs={{1,0},{3,2},{5,4},{7,6},{9,8},{11,10},{13,12},{15,14},{17,16},{19,... | collective-permute-start | bytes 61448 | tf_op jit(solution)/shard_map/ppermute | solution.py:47
  35.7 10.3 %copy-start.1 = (f32[3,4,4,128]{3,2,1,0:T(4,128)S(1)}, f32[3,4,4,128]{3,2,1,0:T(4,128)}, u32[]{:S(2)}) copy-start(f32[3,4,4,128]{3,2,1,0:T(4,128)} %param.77) | copy-start | bytes 73732
  35.7 10.3 %copy-start.5 = (s32[1,1,256]{2,1,0:T(1,128)S(1)}, s32[1,1,256]{2,1,0:T(1,128)}, u32[]{:S(2)}) copy-start(s32[1,1,256]{2,1,0:T(1,128)} %param.81) | copy-start | bytes 3076
  47.3 13.8 %copy-start = (f32[24,24]{1,0:T(8,128)S(1)}, f32[24,24]{1,0:T(8,128)}, u32[]{:S(2)}) copy-start(f32[24,24]{1,0:T(8,128)} %param.80) | copy-start | bytes 6916
  47.6 4.5 %collective-permute-start.4 = (f32[4,1,4,128]{3,0,2,1:T(4,128)S(1)}, f32[4,1,4,128]{3,0,2,1:T(4,128)S(1)}, u32[]{:S(2)}, u32[]{:S(2)}) collective-permute-start(f32[4,1,4,128]{3,0,2,1:T(4,128)S(1)} %get-tuple-element.555), channel_id=1, source_target_pairs={{0,2},{2,4},{4,6},{1,3},{3,5},{5,7},{8,10},{10,12},{12,14},{9,11},... | collective-permute-start | bytes 24584 | tf_op jit(solution)/shard_map/ppermute | solution.py:45
  50.8 4.4 %collective-permute-start.5 = (f32[4,1,4,128]{3,0,2,1:T(4,128)S(1)}, f32[4,1,4,128]{3,0,2,1:T(4,128)S(1)}, u32[]{:S(2)}, u32[]{:S(2)}) collective-permute-start(f32[4,1,4,128]{3,0,2,1:T(4,128)S(1)} %get-tuple-element.556), channel_id=1, source_target_pairs={{2,0},{4,2},{6,4},{3,1},{5,3},{7,5},{10,8},{12,10},{14,12},{11,9},... | collective-permute-start | bytes 24584 | tf_op jit(solution)/shard_map/ppermute | solution.py:47
  55.2 3.5 %collective-permute-start.6 = (f32[4,6,1,128]{3,0,2,1:T(4,128)S(1)}, f32[4,6,1,128]{3,0,2,1:T(4,128)S(1)}, u32[]{:S(2)}, u32[]{:S(2)}) collective-permute-start(f32[4,6,1,128]{3,0,2,1:T(4,128)S(1)} %get-tuple-element.549), channel_id=1, source_target_pairs={{0,1},{2,3},{4,5},{6,7},{8,9},{10,11},{12,13},{14,15},{16,17},{18,... | collective-permute-start | bytes 36872 | tf_op jit(solution)/shard_map/ppermute | solution.py:45
  56.5 4.4 %collective-permute-start.7 = (f32[4,6,1,128]{3,0,2,1:T(4,128)S(1)}, f32[4,6,1,128]{3,0,2,1:T(4,128)S(1)}, u32[]{:S(2)}, u32[]{:S(2)}) collective-permute-start(f32[4,6,1,128]{3,0,2,1:T(4,128)S(1)} %get-tuple-element.550), channel_id=1, source_target_pairs={{1,0},{3,2},{5,4},{7,6},{9,8},{11,10},{13,12},{15,14},{17,16},{19,... | collective-permute-start | bytes 36872 | tf_op jit(solution)/shard_map/ppermute | solution.py:47
  128.8 3.4 %collective-permute-start.8 = (f32[4,1,4,128]{3,2,1,0:T(4,128)S(1)}, f32[4,1,4,128]{3,2,1,0:T(4,128)S(1)}, u32[]{:S(2)}, u32[]{:S(2)}) collective-permute-start(f32[4,1,4,128]{3,2,1,0:T(4,128)S(1)} %get-tuple-element.562), channel_id=1, source_target_pairs={{0,2},{2,4},{4,6},{1,3},{3,5},{5,7},{8,10},{10,12},{12,14},{9,11},... | collective-permute-start | bytes 24584 | tf_op jit(solution)/shard_map/ppermute | solution.py:45
  130.9 4.4 %collective-permute-start.9 = (f32[4,1,4,128]{3,2,1,0:T(4,128)S(1)}, f32[4,1,4,128]{3,2,1,0:T(4,128)S(1)}, u32[]{:S(2)}, u32[]{:S(2)}) collective-permute-start(f32[4,1,4,128]{3,2,1,0:T(4,128)S(1)} %get-tuple-element.563), channel_id=1, source_target_pairs={{2,0},{4,2},{6,4},{3,1},{5,3},{7,5},{10,8},{12,10},{14,12},{11,9},... | collective-permute-start | bytes 24584 | tf_op jit(solution)/shard_map/ppermute | solution.py:47
  135.3 3.9 %collective-permute-start.10 = (f32[4,6,1,128]{3,2,1,0:T(1,128)S(1)}, f32[4,6,1,128]{3,2,1,0:T(1,128)S(1)}, u32[]{:S(2)}, u32[]{:S(2)}) collective-permute-start(f32[4,6,1,128]{3,2,1,0:T(1,128)S(1)} %get-tuple-element.553), channel_id=1, source_target_pairs={{0,1},{2,3},{4,5},{6,7},{8,9},{10,11},{12,13},{14,15},{16,17},{18,... | collective-permute-start | bytes 36872 | tf_op jit(solution)/shard_map/ppermute | solution.py:45
  137.9 4.4 %collective-permute-start.11 = (f32[4,6,1,128]{3,2,1,0:T(1,128)S(1)}, f32[4,6,1,128]{3,2,1,0:T(1,128)S(1)}, u32[]{:S(2)}, u32[]{:S(2)}) collective-permute-start(f32[4,6,1,128]{3,2,1,0:T(1,128)S(1)} %get-tuple-element.554), channel_id=1, source_target_pairs={{1,0},{3,2},{5,4},{7,6},{9,8},{11,10},{13,12},{15,14},{17,16},{19,... | collective-permute-start | bytes 36872 | tf_op jit(solution)/shard_map/ppermute | solution.py:47
  203.7 3.5 %collective-permute-start.12 = (f32[4,1,4,128]{3,2,1,0:T(4,128)S(1)}, f32[4,1,4,128]{3,2,1,0:T(4,128)S(1)}, u32[]{:S(2)}, u32[]{:S(2)}) collective-permute-start(f32[4,1,4,128]{3,2,1,0:T(4,128)S(1)} %get-tuple-element.560), channel_id=1, source_target_pairs={{0,2},{2,4},{4,6},{1,3},{3,5},{5,7},{8,10},{10,12},{12,14},{9,11},... | collective-permute-start | bytes 24584 | tf_op jit(solution)/shard_map/ppermute | solution.py:45
  205.9 4.4 %collective-permute-start.13 = (f32[4,1,4,128]{3,2,1,0:T(4,128)S(1)}, f32[4,1,4,128]{3,2,1,0:T(4,128)S(1)}, u32[]{:S(2)}, u32[]{:S(2)}) collective-permute-start(f32[4,1,4,128]{3,2,1,0:T(4,128)S(1)} %get-tuple-element.561), channel_id=1, source_target_pairs={{2,0},{4,2},{6,4},{3,1},{5,3},{7,5},{10,8},{12,10},{14,12},{11,9},... | collective-permute-start | bytes 24584 | tf_op jit(solution)/shard_map/ppermute | solution.py:47
  210.4 3.8 %collective-permute-start.14 = (f32[4,6,1,128]{3,2,1,0:T(1,128)S(1)}, f32[4,6,1,128]{3,2,1,0:T(1,128)S(1)}, u32[]{:S(2)}, u32[]{:S(2)}) collective-permute-start(f32[4,6,1,128]{3,2,1,0:T(1,128)S(1)} %get-tuple-element.551), channel_id=1, source_target_pairs={{0,1},{2,3},{4,5},{6,7},{8,9},{10,11},{12,13},{14,15},{16,17},{18,... | collective-permute-start | bytes 36872 | tf_op jit(solution)/shard_map/ppermute | solution.py:45
  212.9 4.4 %collective-permute-start.15 = (f32[4,6,1,128]{3,2,1,0:T(1,128)S(1)}, f32[4,6,1,128]{3,2,1,0:T(1,128)S(1)}, u32[]{:S(2)}, u32[]{:S(2)}) collective-permute-start(f32[4,6,1,128]{3,2,1,0:T(1,128)S(1)} %get-tuple-element.552), channel_id=1, source_target_pairs={{1,0},{3,2},{5,4},{7,6},{9,8},{11,10},{13,12},{15,14},{17,16},{19,... | collective-permute-start | bytes 36872 | tf_op jit(solution)/shard_map/ppermute | solution.py:47
  279.8 7.4 %collective-permute-start.16 = (f32[4,3,128]{2,1,0:T(4,128)S(1)}, f32[4,3,128]{2,1,0:T(4,128)S(1)}, u32[]{:S(2)}, u32[]{:S(2)}) collective-permute-start(f32[4,3,128]{2,1,0:T(4,128)S(1)} %get-tuple-element.557), channel_id=1, source_target_pairs={{0,8},{8,16},{16,24},{24,0},{1,9},{9,17},{17,25},{25,1},{2,10},{10... | collective-permute-start | bytes 18440 | tf_op jit(solution)/shard_map/ppermute | solution.py:57
  283.1 4.5 %collective-permute-start.17 = (f32[4,3,128]{2,1,0:T(4,128)S(1)}, f32[4,3,128]{2,1,0:T(4,128)S(1)}, u32[]{:S(2)}, u32[]{:S(2)}) collective-permute-start(f32[4,3,128]{2,1,0:T(4,128)S(1)} %get-tuple-element.559), channel_id=1, source_target_pairs={{0,16},{8,24},{16,0},{24,8},{1,17},{9,25},{17,1},{25,9},{2,18},{10... | collective-permute-start | bytes 18440 | tf_op jit(solution)/shard_map/ppermute | solution.py:57
  286.4 3.1 %collective-permute-start.18 = (f32[4,3,128]{2,1,0:T(4,128)S(1)}, f32[4,3,128]{2,1,0:T(4,128)S(1)}, u32[]{:S(2)}, u32[]{:S(2)}) collective-permute-start(f32[4,3,128]{2,1,0:T(4,128)S(1)} %get-tuple-element.558), channel_id=1, source_target_pairs={{0,24},{8,0},{16,8},{24,16},{1,25},{9,1},{17,9},{25,17},{2,26},{10... | collective-permute-start | bytes 18440 | tf_op jit(solution)/shard_map/ppermute | solution.py:57
  (3 other events, 21.3 us)
where the time goes:
time: 308 us; the launch traced here: 307 us
  blocking collectives  185 us (60%)
  starting transfers between devices  41.9 us (14%)
  other arithmetic  37.4 us (12%)
  waiting for transfers between devices  24.6 us (8%)
  between operations  11 us (4%)
  local copies, waits for them, and re-layouts  6.67 us (2%)
    psum x3, blocking collectives, global_products(): lax.psum((jnp.sum(first_vec * first_vec), jnp.sum(first_vec * second_vec)...  177 us
    cond x36, other arithmetic  23.8 us
    ppermute x8, waiting for transfers between devices, padded(): lax.ppermute(head, axis, [((i + 1) % count, i) for i in range(ends)])  22.2 us
    ppermute x8, starting transfers between devices, padded(): lax.ppermute(tail, axis, [(i, (i + 1) % count) for i in range(ends)])  21 us
    ppermute x8, starting transfers between devices, padded(): lax.ppermute(head, axis, [((i + 1) % count, i) for i in range(ends)])  13.6 us
    all_gather x1, blocking collectives, per_device(): received = lax.all_gather(packed, 'group', axis=0, tiled=True)  7.8 us
    ppermute x3, starting transfers between devices, passed_along(): return lax.ppermute(value, axis, pairs)  7.38 us
  transfers between devices with their start and end apart: 19, of which 10 were waited for; matrix products, arithmetic and copies ran while one was open for 0% of the time, Pallas kernels for 0%

commit v1 on v0

--- a/solution.py
+++ b/solution.py
@@ -34,6 +34,14 @@
 mass_shift = 0.5
 
 
+def mix_the_view(slab_in):
+    mesh_ax = "group"
+    along_axis = ("gx", "gy")
+    for d in (along_axis, mesh_ax):
+        slab_in = lax.psum(slab_in, axis_name=d)
+    return slab_in
+
+
 def padded(cells, sides, width):
     for axis, dim in sides:
         count = lax.axis_size(axis)
@@ -214,9 +222,7 @@
 
 
 def global_products(first_vec, second_vec):
-    return lax.psum(
-        (jnp.sum(first_vec * first_vec), jnp.sum(first_vec * second_vec)), ("group", "gx", "gy")
-    )
+    return mix_the_view((jnp.sum(first_vec * first_vec), jnp.sum(first_vec * second_vec)))
 
 
 def solve_structure(right_side, operator, products):

time: 308 us -> 254 us (0.82)
  blocking collectives: 185 us -> 131 us
    psum x3 -> x6, blocking collectives: 177 us -> 123 us  [mix_the_view(): slab_in = lax.psum(slab_in, axis_name=d)]
where the time goes in v1:
time: 254 us; the launch traced here: 253 us
  blocking collectives  131 us (52%)
  starting transfers between devices  41.6 us (16%)
  other arithmetic  37.4 us (15%)
  waiting for transfers between devices  24.6 us (10%)
  between operations  11.1 us (4%)
  local copies, waits for them, and re-layouts  6.64 us (3%)
    psum x6, blocking collectives, mix_the_view(): slab_in = lax.psum(slab_in, axis_name=d)  123 us
    cond x36, other arithmetic  23.8 us
    ppermute x8, waiting for transfers between devices, padded(): lax.ppermute(head, axis, [((i + 1) % count, i) for i in range(ends)])  22.2 us
    ppermute x8, starting transfers between devices, padded(): lax.ppermute(tail, axis, [(i, (i + 1) % count) for i in range(ends)])  20 us
    ppermute x8, starting transfers between devices, padded(): lax.ppermute(head, axis, [((i + 1) % count, i) for i in range(ends)])  13.6 us
    ppermute x3, starting transfers between devices, passed_along(): return lax.ppermute(value, axis, pairs)  8.14 us
    all_gather x1, blocking collectives, per_device(): received = lax.all_gather(packed, 'group', axis=0, tiled=True)  7.8 us
  transfers between devices with their start and end apart: 19, of which 10 were waited for; matrix products, arithmetic and copies ran while one was open for 0% of the time, Pallas kernels for 0%

profile of v1, /device:TPU:1, one launch (start us, length us, event | category | flops | bytes accessed | tf_op | source)
XLA Modules:
  0.0 252.5 jit_solution(17072028223877614657)
XLA Ops:
  1.4 13.3 %conditional.8 = (bf16[19,2,8,128]{3,2,1,0:T(8,128)(2,1)}) conditional(s32[]{:T(128)} %convert_element_type.59, () %tuple.155, (bf16[19,2,8,128]{3,2,1,0:T(8,128)(2,1)}) %tuple.170), branch_computations={%region_0.1_spmd, %region_1.3_spmd} | conditional | flops 724991 | bytes 1282056 | solution.py:273
  15.5 4.0 %collective-permute-start = (bf16[20,1,8,128]{3,2,1,0:T(8,128)(2,1)S(1)}, bf16[20,1,8,128]{3,2,1,0:T(8,128)(2,1)S(1)}, u32[]{:S(2)}, u32[]{:S(2)}) collective-permute-start(bf16[20,1,8,128]{3,2,1,0:T(8,128)(2,1)S(1)} %get-tuple-element.553), channel_id=1, source_target_pairs={{0,2},{2,4},{4,6},{6,8},{8,10},{10,12},{12,14},{14,16},{16,18},{18... | collective-permute-start | bytes 122888 | tf_op jit(solution)/shard_map/ppermute | solution.py:53
  19.5 4.5 %collective-permute-start.1 = (bf16[20,1,8,128]{3,2,1,0:T(8,128)(2,1)S(1)}, bf16[20,1,8,128]{3,2,1,0:T(8,128)(2,1)S(1)}, u32[]{:S(2)}, u32[]{:S(2)}) collective-permute-start(bf16[20,1,8,128]{3,2,1,0:T(8,128)(2,1)S(1)} %get-tuple-element.554), channel_id=1, source_target_pairs={{2,0},{4,2},{6,4},{8,6},{10,8},{12,10},{14,12},{16,14},{18,16},{20... | collective-permute-start | bytes 122888 | tf_op jit(solution)/shard_map/ppermute | solution.py:55
  26.2 3.1 %collective-permute-start.2 = (bf16[20,4,1,128]{3,2,1,0:T(2,128)(2,1)S(1)}, bf16[20,4,1,128]{3,2,1,0:T(2,128)(2,1)S(1)}, u32[]{:S(2)}, u32[]{:S(2)}) collective-permute-start(bf16[20,4,1,128]{3,2,1,0:T(2,128)(2,1)S(1)} %get-tuple-element.551), channel_id=1, source_target_pairs={{0,1},{2,3},{4,5},{6,7},{8,9},{10,11},{12,13},{14,15},{16,17},{18,... | collective-permute-start | bytes 61448 | tf_op jit(solution)/shard_map/ppermute | solution.py:53
  30.6 3.4 %collective-permute-done.3 = bf16[20,4,1,128]{3,2,1,0:T(2,128)(2,1)S(1)} collective-permute-done((bf16[20,4,1,128]{3,2,1,0:T(2,128)(2,1)S(1)}, bf16[20,4,1,128]{3,2,1,0:T(2,128)(2,1)S(1)}, u32[]{:S(2)}, u32[]{:S(2)}) %collective-permute-start.3) | collective-permute-done | bytes 20512 | tf_op jit(solution)/shard_map/ppermute | solution.py:55
  38.2 7.8 %all_gather.3 = f32[16,6,128]{2,1,0:T(8,128)S(1)} all-gather(f32[4,6,128]{2,1,0:T(8,128)S(1)} %copy.69), channel_id=1, replica_groups=mesh['group'=4,'gx'=4,'gy'=2] {'group'}, dimensions={0}, use_global_device_ids=true | all-gather | bytes 61440 | tf_op jit(solution)/shard_map/all_gather | solution.py:313
  47.6 3.2 %collective-permute-start.4 = (f32[4,1,4,128]{3,0,2,1:T(4,128)S(1)}, f32[4,1,4,128]{3,0,2,1:T(4,128)S(1)}, u32[]{:S(2)}, u32[]{:S(2)}) collective-permute-start(f32[4,1,4,128]{3,0,2,1:T(4,128)S(1)} %get-tuple-element.561), channel_id=1, source_target_pairs={{0,2},{2,4},{4,6},{1,3},{3,5},{5,7},{8,10},{10,12},{12,14},{9,11},... | collective-permute-start | bytes 24584 | tf_op jit(solution)/shard_map/ppermute | solution.py:53
  52.1 3.1 %collective-permute-done.5 = f32[4,1,4,128]{3,0,2,1:T(4,128)S(1)} collective-permute-done((f32[4,1,4,128]{3,0,2,1:T(4,128)S(1)}, f32[4,1,4,128]{3,0,2,1:T(4,128)S(1)}, u32[]{:S(2)}, u32[]{:S(2)}) %collective-permute-start.5) | collective-permute-done | bytes 8224 | tf_op jit(solution)/shard_map/ppermute | solution.py:55
  62.0 15.3 %all-reduce.9 = (f32[]{:T(128)}, f32[]{:T(128)}) all-reduce(f32[]{:T(128)} %multiply_reduce_fusion, f32[]{:T(128)} %multiply_reduce_fusion.1), channel_id=1, replica_groups=mesh['group'=4,'gx'=4,'gy'=2] {'gx','gy'}, use_global_device_ids=true, to_apply=%region_11.12 | all-reduce | flops 2 | bytes 16 | tf_op jit(solution)/shard_map/psum | solution.py:41
  77.3 32.7 %all-reduce.12 = (f32[]{:T(128)}, f32[]{:T(128)}) all-reduce(f32[]{:T(128)} %get-tuple-element.483, f32[]{:T(128)} %get-tuple-element.484), channel_id=1, replica_groups=mesh['group'=4,'gx'=4,'gy'=2] {'group'}, use_global_device_ids=true, to_apply=%region_12.13 | all-reduce | flops 2 | bytes 16 | tf_op jit(solution)/shard_map/psum | solution.py:41
  114.0 3.1 %collective-permute-done.9 = f32[4,1,4,128]{3,2,1,0:T(4,128)S(1)} collective-permute-done((f32[4,1,4,128]{3,2,1,0:T(4,128)S(1)}, f32[4,1,4,128]{3,2,1,0:T(4,128)S(1)}, u32[]{:S(2)}, u32[]{:S(2)}) %collective-permute-start.9) | collective-permute-done | bytes 8224 | tf_op jit(solution)/shard_map/ppermute | solution.py:55
  117.1 2.5 collective-permute-start.10
  121.0 3.1 %collective-permute-done.11 = f32[4,6,1,128]{3,2,1,0:T(1,128)S(1)} collective-permute-done((f32[4,6,1,128]{3,2,1,0:T(1,128)S(1)}, f32[4,6,1,128]{3,2,1,0:T(1,128)S(1)}, u32[]{:S(2)}, u32[]{:S(2)}) %collective-permute-start.11) | collective-permute-done | bytes 12320 | tf_op jit(solution)/shard_map/ppermute | solution.py:55
  125.0 14.5 %all-reduce.8 = (f32[]{:T(128)}, f32[]{:T(128)}) all-reduce(f32[]{:T(128)} %get-tuple-element.478, f32[]{:T(128)} %get-tuple-element.477), channel_id=1, replica_groups=mesh['group'=4,'gx'=4,'gy'=2] {'gx','gy'}, use_global_device_ids=true, to_apply=%region_19.20 | all-reduce | flops 2 | bytes 16 | tf_op jit(solution)/shard_map/psum | solution.py:41
  139.5 23.0 %all-reduce.11 = (f32[]{:T(128)}, f32[]{:T(128)}) all-reduce(f32[]{:T(128)} %get-tuple-element.481, f32[]{:T(128)} %get-tuple-element.482), channel_id=1, replica_groups=mesh['group'=4,'gx'=4,'gy'=2] {'group'}, use_global_device_ids=true, to_apply=%region_20.21 | all-reduce | flops 2 | bytes 16 | tf_op jit(solution)/shard_map/psum | solution.py:41
  169.8 3.1 %collective-permute-done.13 = f32[4,1,4,128]{3,2,1,0:T(4,128)S(1)} collective-permute-done((f32[4,1,4,128]{3,2,1,0:T(4,128)S(1)}, f32[4,1,4,128]{3,2,1,0:T(4,128)S(1)}, u32[]{:S(2)}, u32[]{:S(2)}) %collective-permute-start.13) | collective-permute-done | bytes 8224 | tf_op jit(solution)/shard_map/ppermute | solution.py:55
  172.9 3.2 %collective-permute-start.14 = (f32[4,6,1,128]{3,2,1,0:T(1,128)S(1)}, f32[4,6,1,128]{3,2,1,0:T(1,128)S(1)}, u32[]{:S(2)}, u32[]{:S(2)}) collective-permute-start(f32[4,6,1,128]{3,2,1,0:T(1,128)S(1)} %get-tuple-element.557), channel_id=1, source_target_pairs={{0,1},{2,3},{4,5},{6,7},{8,9},{10,11},{12,13},{14,15},{16,17},{18,... | collective-permute-start | bytes 36872 | tf_op jit(solution)/shard_map/ppermute | solution.py:53
  177.5 3.1 %collective-permute-done.15 = f32[4,6,1,128]{3,2,1,0:T(1,128)S(1)} collective-permute-done((f32[4,6,1,128]{3,2,1,0:T(1,128)S(1)}, f32[4,6,1,128]{3,2,1,0:T(1,128)S(1)}, u32[]{:S(2)}, u32[]{:S(2)}) %collective-permute-start.15) | collective-permute-done | bytes 12320 | tf_op jit(solution)/shard_map/ppermute | solution.py:55
  181.3 14.4 %all-reduce.7 = (f32[]{:T(128)}, f32[]{:T(128)}) all-reduce(f32[]{:T(128)} %get-tuple-element.476, f32[]{:T(128)} %get-tuple-element.475), channel_id=1, replica_groups=mesh['group'=4,'gx'=4,'gy'=2] {'gx','gy'}, use_global_device_ids=true, to_apply=%region_27.28 | all-reduce | flops 2 | bytes 16 | tf_op jit(solution)/shard_map/psum | solution.py:41
  195.7 23.0 %all-reduce.10 = (f32[]{:T(128)}, f32[]{:T(128)}) all-reduce(f32[]{:T(128)} %get-tuple-element.479, f32[]{:T(128)} %get-tuple-element.480), channel_id=1, replica_groups=mesh['group'=4,'gx'=4,'gy'=2] {'group'}, use_global_device_ids=true, to_apply=%region_28.29 | all-reduce | flops 2 | bytes 16 | tf_op jit(solution)/shard_map/psum | solution.py:41
  224.7 2.3 collective-permute-start.16
  227.0 5.1 %collective-permute-start.17 = (f32[4,3,128]{2,1,0:T(4,128)S(1)}, f32[4,3,128]{2,1,0:T(4,128)S(1)}, u32[]{:S(2)}, u32[]{:S(2)}) collective-permute-start(f32[4,3,128]{2,1,0:T(4,128)S(1)} %get-tuple-element.565), channel_id=1, source_target_pairs={{0,16},{8,24},{16,0},{24,8},{1,17},{9,25},{17,1},{25,9},{2,18},{10... | collective-permute-start | bytes 18440 | tf_op jit(solution)/shard_map/ppermute | solution.py:65
  235.3 2.5 scatter_custom_fusion.3
  237.9 14.7 %conditional.15 = (bf16[19,2,8,128]{3,2,1,0:T(8,128)(2,1)}) conditional(s32[]{:T(128)} %convert_element_type.59, () %tuple.154, (f32[4,10,130]{2,1,0:T(8,128)S(1)}, f32[19,4,10,130]{3,2,1,0:T(8,128)S(1)}, f32[3,2048]{0,1:T(8,128)S(1)}) %tuple.168), branch_computations={%region_38.39_spmd, %region_39.40_spmd} | conditional | flops 356351 | bytes 1826696 | solution.py:362
  (138 shorter events, 65.0 us)
Async XLA Ops:
  0.6 30.0 %copy-start.3 = (f32[4,4,128]{2,1,0:T(4,128)S(1)}, f32[4,4,128]{2,1,0:T(4,128)}, u32[]{:S(2)}) copy-start(f32[4,4,128]{2,1,0:T(4,128)} %param.78) | copy-start | bytes 24580
  0.6 30.0 %copy-start.4 = (s32[4,4,128]{2,1,0:T(4,128)S(1)}, s32[4,4,128]{2,1,0:T(4,128)}, u32[]{:S(2)}) copy-start(s32[4,4,128]{2,1,0:T(4,128)} %param.79) | copy-start | bytes 24580
  15.5 8.6 %collective-permute-start = (bf16[20,1,8,128]{3,2,1,0:T(8,128)(2,1)S(1)}, bf16[20,1,8,128]{3,2,1,0:T(8,128)(2,1)S(1)}, u32[]{:S(2)}, u32[]{:S(2)}) collective-permute-start(bf16[20,1,8,128]{3,2,1,0:T(8,128)(2,1)S(1)} %get-tuple-element.553), channel_id=1, source_target_pairs={{0,2},{2,4},{4,6},{6,8},{8,10},{10,12},{12,14},{14,16},{16,18},{18... | collective-permute-start | bytes 122888 | tf_op jit(solution)/shard_map/ppermute | solution.py:53
  19.5 5.6 %collective-permute-start.1 = (bf16[20,1,8,128]{3,2,1,0:T(8,128)(2,1)S(1)}, bf16[20,1,8,128]{3,2,1,0:T(8,128)(2,1)S(1)}, u32[]{:S(2)}, u32[]{:S(2)}) collective-permute-start(bf16[20,1,8,128]{3,2,1,0:T(8,128)(2,1)S(1)} %get-tuple-element.554), channel_id=1, source_target_pairs={{2,0},{4,2},{6,4},{8,6},{10,8},{12,10},{14,12},{16,14},{18,16},{20... | collective-permute-start | bytes 122888 | tf_op jit(solution)/shard_map/ppermute | solution.py:55
  26.2 4.5 %collective-permute-start.2 = (bf16[20,4,1,128]{3,2,1,0:T(2,128)(2,1)S(1)}, bf16[20,4,1,128]{3,2,1,0:T(2,128)(2,1)S(1)}, u32[]{:S(2)}, u32[]{:S(2)}) collective-permute-start(bf16[20,4,1,128]{3,2,1,0:T(2,128)(2,1)S(1)} %get-tuple-element.551), channel_id=1, source_target_pairs={{0,1},{2,3},{4,5},{6,7},{8,9},{10,11},{12,13},{14,15},{16,17},{18,... | collective-permute-start | bytes 61448 | tf_op jit(solution)/shard_map/ppermute | solution.py:53
  29.3 4.7 %collective-permute-start.3 = (bf16[20,4,1,128]{3,2,1,0:T(2,128)(2,1)S(1)}, bf16[20,4,1,128]{3,2,1,0:T(2,128)(2,1)S(1)}, u32[]{:S(2)}, u32[]{:S(2)}) collective-permute-start(bf16[20,4,1,128]{3,2,1,0:T(2,128)(2,1)S(1)} %get-tuple-element.552), channel_id=1, source_target_pairs={{1,0},{3,2},{5,4},{7,6},{9,8},{11,10},{13,12},{15,14},{17,16},{19,... | collective-permute-start | bytes 61448 | tf_op jit(solution)/shard_map/ppermute | solution.py:55
  35.7 10.3 %copy-start.1 = (f32[3,4,4,128]{3,2,1,0:T(4,128)S(1)}, f32[3,4,4,128]{3,2,1,0:T(4,128)}, u32[]{:S(2)}) copy-start(f32[3,4,4,128]{3,2,1,0:T(4,128)} %param.77) | copy-start | bytes 73732
  35.7 10.3 %copy-start.5 = (s32[1,1,256]{2,1,0:T(1,128)S(1)}, s32[1,1,256]{2,1,0:T(1,128)}, u32[]{:S(2)}) copy-start(s32[1,1,256]{2,1,0:T(1,128)} %param.81) | copy-start | bytes 3076
  47.3 13.8 %copy-start = (f32[24,24]{1,0:T(8,128)S(1)}, f32[24,24]{1,0:T(8,128)}, u32[]{:S(2)}) copy-start(f32[24,24]{1,0:T(8,128)} %param.80) | copy-start | bytes 6916
  47.6 4.5 %collective-permute-start.4 = (f32[4,1,4,128]{3,0,2,1:T(4,128)S(1)}, f32[4,1,4,128]{3,0,2,1:T(4,128)S(1)}, u32[]{:S(2)}, u32[]{:S(2)}) collective-permute-start(f32[4,1,4,128]{3,0,2,1:T(4,128)S(1)} %get-tuple-element.561), channel_id=1, source_target_pairs={{0,2},{2,4},{4,6},{1,3},{3,5},{5,7},{8,10},{10,12},{12,14},{9,11},... | collective-permute-start | bytes 24584 | tf_op jit(solution)/shard_map/ppermute | solution.py:53
  50.8 4.4 %collective-permute-start.5 = (f32[4,1,4,128]{3,0,2,1:T(4,128)S(1)}, f32[4,1,4,128]{3,0,2,1:T(4,128)S(1)}, u32[]{:S(2)}, u32[]{:S(2)}) collective-permute-start(f32[4,1,4,128]{3,0,2,1:T(4,128)S(1)} %get-tuple-element.562), channel_id=1, source_target_pairs={{2,0},{4,2},{6,4},{3,1},{5,3},{7,5},{10,8},{12,10},{14,12},{11,9},... | collective-permute-start | bytes 24584 | tf_op jit(solution)/shard_map/ppermute | solution.py:55
  55.2 3.5 %collective-permute-start.6 = (f32[4,6,1,128]{3,0,2,1:T(4,128)S(1)}, f32[4,6,1,128]{3,0,2,1:T(4,128)S(1)}, u32[]{:S(2)}, u32[]{:S(2)}) collective-permute-start(f32[4,6,1,128]{3,0,2,1:T(4,128)S(1)} %get-tuple-element.555), channel_id=1, source_target_pairs={{0,1},{2,3},{4,5},{6,7},{8,9},{10,11},{12,13},{14,15},{16,17},{18,... | collective-permute-start | bytes 36872 | tf_op jit(solution)/shard_map/ppermute | solution.py:53
  56.5 4.4 %collective-permute-start.7 = (f32[4,6,1,128]{3,0,2,1:T(4,128)S(1)}, f32[4,6,1,128]{3,0,2,1:T(4,128)S(1)}, u32[]{:S(2)}, u32[]{:S(2)}) collective-permute-start(f32[4,6,1,128]{3,0,2,1:T(4,128)S(1)} %get-tuple-element.556), channel_id=1, source_target_pairs={{1,0},{3,2},{5,4},{7,6},{9,8},{11,10},{13,12},{15,14},{17,16},{19,... | collective-permute-start | bytes 36872 | tf_op jit(solution)/shard_map/ppermute | solution.py:55
  111.4 2.6 %collective-permute-start.8 = (f32[4,1,4,128]{3,2,1,0:T(4,128)S(1)}, f32[4,1,4,128]{3,2,1,0:T(4,128)S(1)}, u32[]{:S(2)}, u32[]{:S(2)}) collective-permute-start(f32[4,1,4,128]{3,2,1,0:T(4,128)S(1)} %get-tuple-element.568), channel_id=1, source_target_pairs={{0,2},{2,4},{4,6},{1,3},{3,5},{5,7},{8,10},{10,12},{12,14},{9,11},... | collective-permute-start | bytes 24584 | tf_op jit(solution)/shard_map/ppermute | solution.py:53
  112.7 4.4 %collective-permute-start.9 = (f32[4,1,4,128]{3,2,1,0:T(4,128)S(1)}, f32[4,1,4,128]{3,2,1,0:T(4,128)S(1)}, u32[]{:S(2)}, u32[]{:S(2)}) collective-permute-start(f32[4,1,4,128]{3,2,1,0:T(4,128)S(1)} %get-tuple-element.569), channel_id=1, source_target_pairs={{2,0},{4,2},{6,4},{3,1},{5,3},{7,5},{10,8},{12,10},{14,12},{11,9},... | collective-permute-start | bytes 24584 | tf_op jit(solution)/shard_map/ppermute | solution.py:55
  117.1 3.8 %collective-permute-start.10 = (f32[4,6,1,128]{3,2,1,0:T(1,128)S(1)}, f32[4,6,1,128]{3,2,1,0:T(1,128)S(1)}, u32[]{:S(2)}, u32[]{:S(2)}) collective-permute-start(f32[4,6,1,128]{3,2,1,0:T(1,128)S(1)} %get-tuple-element.559), channel_id=1, source_target_pairs={{0,1},{2,3},{4,5},{6,7},{8,9},{10,11},{12,13},{14,15},{16,17},{18,... | collective-permute-start | bytes 36872 | tf_op jit(solution)/shard_map/ppermute | solution.py:53
  119.6 4.4 %collective-permute-start.11 = (f32[4,6,1,128]{3,2,1,0:T(1,128)S(1)}, f32[4,6,1,128]{3,2,1,0:T(1,128)S(1)}, u32[]{:S(2)}, u32[]{:S(2)}) collective-permute-start(f32[4,6,1,128]{3,2,1,0:T(1,128)S(1)} %get-tuple-element.560), channel_id=1, source_target_pairs={{1,0},{3,2},{5,4},{7,6},{9,8},{11,10},{13,12},{15,14},{17,16},{19,... | collective-permute-start | bytes 36872 | tf_op jit(solution)/shard_map/ppermute | solution.py:55
  167.2 2.6 %collective-permute-start.12 = (f32[4,1,4,128]{3,2,1,0:T(4,128)S(1)}, f32[4,1,4,128]{3,2,1,0:T(4,128)S(1)}, u32[]{:S(2)}, u32[]{:S(2)}) collective-permute-start(f32[4,1,4,128]{3,2,1,0:T(4,128)S(1)} %get-tuple-element.566), channel_id=1, source_target_pairs={{0,2},{2,4},{4,6},{1,3},{3,5},{5,7},{8,10},{10,12},{12,14},{9,11},... | collective-permute-start | bytes 24584 | tf_op jit(solution)/shard_map/ppermute | solution.py:53
  168.5 4.4 %collective-permute-start.13 = (f32[4,1,4,128]{3,2,1,0:T(4,128)S(1)}, f32[4,1,4,128]{3,2,1,0:T(4,128)S(1)}, u32[]{:S(2)}, u32[]{:S(2)}) collective-permute-start(f32[4,1,4,128]{3,2,1,0:T(4,128)S(1)} %get-tuple-element.567), channel_id=1, source_target_pairs={{2,0},{4,2},{6,4},{3,1},{5,3},{7,5},{10,8},{12,10},{14,12},{11,9},... | collective-permute-start | bytes 24584 | tf_op jit(solution)/shard_map/ppermute | solution.py:55
  172.9 4.6 %collective-permute-start.14 = (f32[4,6,1,128]{3,2,1,0:T(1,128)S(1)}, f32[4,6,1,128]{3,2,1,0:T(1,128)S(1)}, u32[]{:S(2)}, u32[]{:S(2)}) collective-permute-start(f32[4,6,1,128]{3,2,1,0:T(1,128)S(1)} %get-tuple-element.557), channel_id=1, source_target_pairs={{0,1},{2,3},{4,5},{6,7},{8,9},{10,11},{12,13},{14,15},{16,17},{18,... | collective-permute-start | bytes 36872 | tf_op jit(solution)/shard_map/ppermute | solution.py:53
  176.2 4.4 %collective-permute-start.15 = (f32[4,6,1,128]{3,2,1,0:T(1,128)S(1)}, f32[4,6,1,128]{3,2,1,0:T(1,128)S(1)}, u32[]{:S(2)}, u32[]{:S(2)}) collective-permute-start(f32[4,6,1,128]{3,2,1,0:T(1,128)S(1)} %get-tuple-element.558), channel_id=1, source_target_pairs={{1,0},{3,2},{5,4},{7,6},{9,8},{11,10},{13,12},{15,14},{17,16},{19,... | collective-permute-start | bytes 36872 | tf_op jit(solution)/shard_map/ppermute | solution.py:55
  224.7 8.1 %collective-permute-start.16 = (f32[4,3,128]{2,1,0:T(4,128)S(1)}, f32[4,3,128]{2,1,0:T(4,128)S(1)}, u32[]{:S(2)}, u32[]{:S(2)}) collective-permute-start(f32[4,3,128]{2,1,0:T(4,128)S(1)} %get-tuple-element.563), channel_id=1, source_target_pairs={{0,8},{8,16},{16,24},{24,0},{1,9},{9,17},{17,25},{25,1},{2,10},{10... | collective-permute-start | bytes 18440 | tf_op jit(solution)/shard_map/ppermute | solution.py:65
  227.0 6.4 %collective-permute-start.17 = (f32[4,3,128]{2,1,0:T(4,128)S(1)}, f32[4,3,128]{2,1,0:T(4,128)S(1)}, u32[]{:S(2)}, u32[]{:S(2)}) collective-permute-start(f32[4,3,128]{2,1,0:T(4,128)S(1)} %get-tuple-element.565), channel_id=1, source_target_pairs={{0,16},{8,24},{16,0},{24,8},{1,17},{9,25},{17,1},{25,9},{2,18},{10... | collective-permute-start | bytes 18440 | tf_op jit(solution)/shard_map/ppermute | solution.py:65
  232.1 3.1 %collective-permute-start.18 = (f32[4,3,128]{2,1,0:T(4,128)S(1)}, f32[4,3,128]{2,1,0:T(4,128)S(1)}, u32[]{:S(2)}, u32[]{:S(2)}) collective-permute-start(f32[4,3,128]{2,1,0:T(4,128)S(1)} %get-tuple-element.564), channel_id=1, source_target_pairs={{0,24},{8,0},{16,8},{24,16},{1,25},{9,1},{17,9},{25,17},{2,26},{10... | collective-permute-start | bytes 18440 | tf_op jit(solution)/shard_map/ppermute | solution.py:65
  (3 other events, 21.2 us)
